TPU v7x, 256 devices: a whole 4x4x8 slice. The times are simulated.
256 devices in a mesh: space: 16 (over x_hi, z), chan: 8 (over y, core), dp: 2 (over x_lo).
Axes of the slice: x: 4 (x_hi: 2, x_lo: 2; x = x_hi * 2 + x_lo), y: 4, z: 8, core: 2. Of those that a mesh axis runs over, the one named last changes fastest.
Arguments:
- inputs: bfloat16 [2, 32, 8, 128, 512], P('dp', 'space', None, 'chan'), may hold values from -6 to 6
- cotangent: bfloat16 [2, 32, 8, 128, 512], P('dp', 'space', None, 'chan'), may hold values from -6 to 6
- weight: bfloat16 [27, 128, 128], P(None, 'chan'), may hold values from -0.109375 to 0.109375
Outputs:
- input_grad: bfloat16 [2, 32, 8, 128, 512], P('dp', 'space', None, 'chan')
- weight_grad: float32 [27, 128, 128], P(None, 'chan')
All inputs are finite; a program needn't handle non-finite values.
Results may differ from a plain program's by a relative error of at most 0.001.
Values may be sent and summed in bfloat16 or wider, within the bound.
No kernel may reach another device: no remote copies, remote signals or barrier semaphores. Data moves between devices by JAX's collectives and lax.ppermute only.
A program may use at most 64 MiB of HBM per device.

v0:
```python
import math
import jax
import jax.numpy as jnp
from jax import lax
from jax.sharding import PartitionSpec as P


def from_behind(value, axis, steps):
    count = lax.axis_size(axis)
    initial, last = (max(0, -steps), min(count, count - steps))
    return lax.ppermute(value, axis, [(source, source + steps) for source in range(initial, last)])


def shift_cells(block, step_z, step_y):
    zero = jnp.zeros((), block.dtype)
    config = ((0, 0, 0), (0, 0, 0), (step_z, -step_z, 0), (0, 0, 0), (step_y, -step_y, 0))
    return lax.pad(block, zero, config)


def local(inputs, cotangent, weight):
    samples, planes, depth, channels, width = inputs.shape
    outputs = weight.shape[2]
    gathered = lax.all_gather(cotangent, "chan", axis=3, tiled=True)
    lower_plane = from_behind(gathered[:, -1:], "space", 1)
    upper_plane = from_behind(gathered[:, :1], "space", -1)
    stacked = jnp.concatenate(
        [shift_cells(inputs, -step_z, -step_y) for step_z in (-1, 0, 1) for step_y in (-1, 0, 1)],
        axis=3,
    )
    accum = jnp.zeros(inputs.shape, jnp.float32)
    groups = []
    for step_x in (-1, 0, 1):
        if step_x == 1:
            slab = jnp.concatenate([lower_plane, gathered[:, : planes - 1]], axis=1)
        elif step_x == -1:
            slab = jnp.concatenate([gathered[:, 1:], upper_plane], axis=1)
        else:
            slab = gathered
        first = 9 * (step_x + 1)
        groups.append(
            jnp.einsum("bxzky,bxzcy->kc", stacked, slab, preferred_element_type=jnp.float32)
        )
        for step_y in (-1, 0, 1):
            kernel = weight[first + step_y + 1 : first + 9 : 3].reshape(3 * channels, outputs)
            product = jnp.einsum(
                "bxzcy,kc->bxzky", slab, kernel, preferred_element_type=jnp.float32
            )
            for place, step_z in enumerate((-1, 0, 1)):
                part = product[:, :, :, place * channels : (place + 1) * channels]
                accum = accum + shift_cells(part, step_z, step_y)
    input_grad = accum.astype(jnp.bfloat16)
    local_grad = jnp.concatenate(groups, axis=0).reshape(27, channels, outputs)
    count = samples * lax.axis_size("dp") * planes * lax.axis_size("space") * depth * width
    scale = 1.0 / math.sqrt(count)
    weight_grad = lax.psum(local_grad, ("space", "dp")) * scale
    return (input_grad, weight_grad)


def solution(mesh):
    placed = (
        P("dp", "space", None, "chan", None),
        P("dp", "space", None, "chan", None),
        P(None, "chan", None),
    )
    return jax.shard_map(
        local,
        mesh=mesh,
        in_specs=placed,
        out_specs=(P("dp", "space", None, "chan", None), P(None, "chan", None)),
        check_vma=False,
    )
```

profile of v0, /device:TPU:2, one launch (start us, length us, event | category | flops | bytes accessed | tf_op | source)
XLA Modules:
  0.0 232.0 jit_solution(5952417123900889191)
XLA Ops:
  7.2 0.0 copy-start.1
  7.2 0.0 all-gather.2.cloned.1.call-start
  7.2 0.7 all-gather.2.cloned.1.call-update
  7.9 0.0 all-reduce.34.cloned.1.call-start
  8.0 1.1 fusion.64
  9.0 0.0 copy-start.21
  9.0 1.0 fusion.60
  10.0 1.1 fusion.65
  11.1 1.1 fusion.62
  12.3 0.1 fusion.63
  12.4 0.1 fusion.66
  12.6 0.1 fusion.67
  12.7 1.4 copy-done.5
  14.2 26.5 %all-gather.2.cloned.1.call-done = bf16[1,2,8,128,512]{4,3,2,1,0:T(8,128)(2,1)} async-done(((bf16[1,2,8,16,512]{4,3,2,1,0:T(8,128)(2,1)}), bf16[1,2,8,128,512]{4,3,2,1,0:T(8,128)(2,1)}) %all-gather.2.cloned.1.call-update) | async-done | bytes 2097168 | tf_op jit(solution)/shard_map/all_gather | solution.py:23
  40.7 1.9 fusion.68
  42.6 3.5 %collective-permute-start.1 = (bf16[1,1,8,128,512]{4,3,2,1,0:T(8,128)(2,1)S(1)}, bf16[1,1,8,128,512]{4,3,2,1,0:T(8,128)(2,1)S(1)}, u32[]{:S(2)}, u32[]{:S(2)}) collective-permute-start(bf16[1,1,8,128,512]{4,3,2,1,0:T(8,128)(2,1)S(1)} %get-tuple-element.2), channel_id=1, source_target_pairs={{0,16},{16,32},{32,48},{48,64},{64,80},{80,96},{96,112},{112,128},... | collective-permute-start | bytes 3145736 | tf_op jit(solution)/shard_map/ppermute | solution.py:11
  46.1 1.3 collective-permute-start
  47.4 0.4 fusion.16
  47.9 0.4 fusion.19
  48.3 0.4 fusion.13
  48.7 0.3 copy-done.4
  49.0 1.5 fusion.72
  50.5 1.2 fusion.74
  51.7 1.1 copy-done.6
  52.8 0.8 fusion.25
  53.5 19.5 %collective-permute-done = bf16[1,1,8,128,512]{4,3,2,1,0:T(8,128)(2,1)S(1)} collective-permute-done((bf16[1,1,8,128,512]{4,3,2,1,0:T(8,128)(2,1)S(1)}, bf16[1,1,8,128,512]{4,3,2,1,0:T(8,128)(2,1)S(1)}, u32[]{:S(2)}, u32[]{:S(2)}) %collective-permute-start) | collective-permute-done | bytes 1048608 | tf_op jit(solution)/shard_map/ppermute | solution.py:11
  73.0 0.4 convolution_bitcast_fusion.3
  73.4 1.2 fusion.71
  74.6 0.0 collective-permute-done.1
  74.6 0.4 convolution_bitcast_fusion
  75.1 1.2 fusion.77
  76.3 0.8 fusion.30
  77.1 0.8 fusion.22
  77.8 0.7 pad_maximum_fusion
  78.5 0.0 all-reduce.34.cloned.1.call-update
  78.6 1.7 convolution_bitcast_fusion.4
  80.3 0.4 convolution_bitcast_fusion.5
  80.8 0.4 fusion.69
  81.1 0.4 convolution_bitcast_fusion.1
  81.6 0.4 convolution_bitcast_fusion.2
  82.0 0.0 copy-start.7
  82.0 0.0 copy-start.8
  82.0 0.0 copy-start.9
  82.0 0.0 copy-start.10
  82.0 0.0 copy-start.11
  82.0 0.0 copy-start.12
  82.1 0.4 fusion.75
  82.5 0.1 copy-done.17
  82.6 0.2 copy-done.18
  82.7 0.2 copy-done.19
  82.9 0.2 copy-done.20
  83.1 0.3 copy-done.7
  83.3 0.2 copy-done.8
  83.5 0.2 copy-done.9
  83.6 0.2 copy-done.10
  83.8 0.2 copy-done.11
  84.0 0.2 copy-done.12
  84.1 0.2 copy-done.13
  84.3 0.2 copy-done.14
  84.4 0.2 copy-done.15
  84.6 0.2 copy-done.16
  84.7 4.3 %fusion.59 = bf16[1,2,8,16,512]{4,3,2,1,0:T(8,128)(2,1)} fusion(f32[1,2,8,16,512]{4,3,2,1,0:T(8,128)S(1)} %copy-done.19, f32[1,2,8,16,512]{4,3,2,1,0:T(8,128)S(1)} %copy-done.20, f32[1,2,8,16,512]{4,3,2,1,0:T(8,128)S(1)} %copy-done.18, f32[1,2,8,16,512]{4,3,2,1,0:T(8,128)S(1)} %get-tuple-element.41, f32[1,2,8,48,512]{4,3,2,1,0:T(8,128)S(1)} %convolution_bitcast_fusion.1, ...), kind=kLoop, calls=%fused_computation.77 | loop fusion | flops 3538944 | bytes 14417920 | tf_op jit(solution)/shard_map/convert_element_type | solution.py:51
  89.0 134.5 %all-reduce.34.cloned.1.call-done = f32[27,16,128]{2,1,0:T(8,128)} async-done(((f32[27,16,128]{2,1,0:T(8,128)}), f32[27,16,128]{2,1,0:T(8,128)}) %all-reduce.34.cloned.1.call-update) | async-done | bytes 221200 | tf_op jit(solution)/shard_map/psum | solution.py:55
  223.5 1.6 broadcast_multiply_fusion
  (22 shorter events, 0.1 us)
Async XLA Ops:
  7.2 5.1 %copy-start.1 = (bf16[1,2,8,16,512]{4,3,2,1,0:T(8,128)(2,1)S(1)}, bf16[1,2,8,16,512]{4,3,2,1,0:T(8,128)(2,1)}, u32[]{:S(2)}) copy-start(bf16[1,2,8,16,512]{4,3,2,1,0:T(8,128)(2,1)} %param.3) | copy-start | bytes 786436
  7.2 33.5 %all-gather.2.cloned.1.call-start = ((), (), s32[]{:S(2)}) async-start(), calls=%async_computation | async-start | bytes 2359296 | tf_op jit(solution)/shard_map/all_gather | solution.py:23
  7.9 215.6 %all-reduce.34.cloned.1.call-start = ((), (), s32[]{:S(2)}) async-start(), calls=%async_computation.1 | async-start | bytes 442368 | tf_op jit(solution)/shard_map/psum | solution.py:55
  9.0 5.1 %copy-start.21 = (bf16[27,16,128]{2,1,0:T(8,128)(2,1)S(1)}, bf16[27,16,128]{2,1,0:T(8,128)(2,1)}, u32[]{:S(2)}) copy-start(bf16[27,16,128]{2,1,0:T(8,128)(2,1)} %param.5) | copy-start | bytes 331780
  12.7 1.4 copy-start.5
  40.7 6.7 %copy-start = (bf16[1,2,8,128,512]{4,3,2,1,0:T(8,128)(2,1)S(1)}, bf16[1,2,8,128,512]{4,3,2,1,0:T(8,128)(2,1)}, u32[]{:S(2)}) copy-start(bf16[1,2,8,128,512]{4,3,2,1,0:T(8,128)(2,1)} %all-gather.2.cloned.1.call-done) | copy-start | bytes 6291460
  42.6 32.1 %collective-permute-start.1 = (bf16[1,1,8,128,512]{4,3,2,1,0:T(8,128)(2,1)S(1)}, bf16[1,1,8,128,512]{4,3,2,1,0:T(8,128)(2,1)S(1)}, u32[]{:S(2)}, u32[]{:S(2)}) collective-permute-start(bf16[1,1,8,128,512]{4,3,2,1,0:T(8,128)(2,1)S(1)} %get-tuple-element.2), channel_id=1, source_target_pairs={{0,16},{16,32},{32,48},{48,64},{64,80},{80,96},{96,112},{112,128},... | collective-permute-start | bytes 3145736 | tf_op jit(solution)/shard_map/ppermute | solution.py:11
  46.1 26.9 %collective-permute-start = (bf16[1,1,8,128,512]{4,3,2,1,0:T(8,128)(2,1)S(1)}, bf16[1,1,8,128,512]{4,3,2,1,0:T(8,128)(2,1)S(1)}, u32[]{:S(2)}, u32[]{:S(2)}) collective-permute-start(bf16[1,1,8,128,512]{4,3,2,1,0:T(8,128)(2,1)S(1)} %get-tuple-element.3), channel_id=1, source_target_pairs={{16,0},{32,16},{48,32},{64,48},{80,64},{96,80},{112,96},{128,112},... | collective-permute-start | bytes 3145736 | tf_op jit(solution)/shard_map/ppermute | solution.py:11
  47.8 1.2 copy-start.4
  50.5 2.2 copy-start.6
  73.0 4.0 %copy-start.2 = (bf16[1,1,8,128,512]{4,3,2,1,0:T(8,128)(2,1)}, bf16[1,1,8,128,512]{4,3,2,1,0:T(8,128)(2,1)S(1)}, u32[]{:S(2)}) copy-start(bf16[1,1,8,128,512]{4,3,2,1,0:T(8,128)(2,1)S(1)} %collective-permute-done) | copy-start | bytes 3145732
  78.6 1.7 copy-start.3
  81.5 1.0 copy-start.17
  81.5 1.2 copy-start.18
  81.6 1.3 copy-start.19
  81.6 1.5 copy-start.20
  82.0 1.3 copy-start.7
  82.0 1.5 copy-start.8
  82.0 1.6 copy-start.9
  82.0 1.8 copy-start.10
  82.0 1.9 copy-start.11
  82.0 2.1 copy-start.12
  82.1 2.2 copy-start.13
  82.1 2.4 %copy-start.14 = (f32[1,2,8,16,512]{4,3,2,1,0:T(8,128)S(1)}, f32[1,2,8,16,512]{4,3,2,1,0:T(8,128)}, u32[]{:S(2)}) copy-start(f32[1,2,8,16,512]{4,3,2,1,0:T(8,128)} %get-tuple-element.19) | copy-start | bytes 1572868
  82.1 2.5 %copy-start.15 = (f32[1,2,8,16,512]{4,3,2,1,0:T(8,128)S(1)}, f32[1,2,8,16,512]{4,3,2,1,0:T(8,128)}, u32[]{:S(2)}) copy-start(f32[1,2,8,16,512]{4,3,2,1,0:T(8,128)} %get-tuple-element.9) | copy-start | bytes 1572868
  82.1 2.7 %copy-start.16 = (f32[1,2,8,16,512]{4,3,2,1,0:T(8,128)S(1)}, f32[1,2,8,16,512]{4,3,2,1,0:T(8,128)}, u32[]{:S(2)}) copy-start(f32[1,2,8,16,512]{4,3,2,1,0:T(8,128)} %get-tuple-element.10) | copy-start | bytes 1572868
Sparse Core Ops, SparseCore 0:
  9.8 30.8 all-gather.1
  78.7 144.8 all-reduce.33
where the time goes:
time: 232 us
  waiting for transfers between devices  181 us (78%)
  local copies, waits for them, and re-layouts  17.5 us (8%)
  between operations  14.4 us (6%)
  matrix products  7.41 us (3%)
  other arithmetic  6.63 us (3%)
  starting transfers between devices  4.89 us (2%)
    psum x1, waiting for transfers between devices, local(): weight_grad = lax.psum(local_grad, ('space', 'dp')) * scale  134 us
    all_gather x1, waiting for transfers between devices, local(): gathered = lax.all_gather(cotangent, 'chan', axis=3, tiled=True)  26.5 us
    ppermute x2, waiting for transfers between devices, from_behind(): lax.ppermute(value, axis, [(source, source + steps) for source in range(i...  19.5 us
    unnamed x52, local copies, waits for them, and re-layouts  9.68 us
    slice x6, local copies, waits for them, and re-layouts, local(): part = product[:, :, :, place * channels:(place + 1) * channels]  5.81 us
    dot_general x9, matrix products, local(): jnp.einsum('bxzcy,kc->bxzky', slab, kernel, preferred_element_type=jnp.fl...  5.09 us
    ppermute x2, starting transfers between devices, from_behind(): lax.ppermute(value, axis, [(source, source + steps) for source in range(i...  4.82 us
  transfers between devices with their start and end apart: 4, of which 3 were waited for; matrix products, arithmetic and copies ran while one was open for 8% of the time, Pallas kernels for 0%

commit v1 on v0

--- a/solution.py
+++ b/solution.py
@@ -3,6 +3,7 @@
 import jax.numpy as jnp
 from jax import lax
 from jax.sharding import PartitionSpec as P
+from jax.lax import all_gather
 
 
 def from_behind(value, axis, steps):
@@ -52,7 +53,8 @@
     local_grad = jnp.concatenate(groups, axis=0).reshape(27, channels, outputs)
     count = samples * lax.axis_size("dp") * planes * lax.axis_size("space") * depth * width
     scale = 1.0 / math.sqrt(count)
-    weight_grad = lax.psum(local_grad, ("space", "dp")) * scale
+    lots_all_handle = lambda state, mesh_ax: all_gather(state, axis_name=mesh_ax).sum(axis=0)
+    weight_grad = lots_all_handle(local_grad, mesh_ax=("space", "dp")) * scale
     return (input_grad, weight_grad)
 
 

time: 232 us -> 256 us (1.10)
  waiting for transfers between devices: 181 us -> 201 us
  matrix products: 7.41 us -> 11.9 us
  local copies, waits for them, and re-layouts: 17.5 us -> 13.8 us
    all_gather x0 -> x1, waiting for transfers between devices: none -> 155 us  [local(): all_gather(state, axis_name=mesh_ax).sum(axis=0)]
    psum x1 -> x0, waiting for transfers between devices: 134 us -> none  [local(): weight_grad = lax.psum(local_grad, ('space', 'dp')) * scale]
    dot_general x3, matrix products: 2.31 us -> 8.07 us  [local(): jnp.einsum('bxzky,bxzcy->kc', stacked, slab, preferred_element_type=jnp.f...]
    slice x6, local copies, waits for them, and re-layouts: 5.81 us -> 1.65 us  [local(): part = product[:, :, :, place * channels:(place + 1) * channels]]
    reduce_sum x0 -> x1, other arithmetic: none -> 3.46 us  [local(): all_gather(state, axis_name=mesh_ax).sum(axis=0)]
    all_gather x1, waiting for transfers between devices: 26.5 us -> 29.3 us  [local(): gathered = lax.all_gather(cotangent, 'chan', axis=3, tiled=True)]
    unnamed x52 -> x26, local copies, waits for them, and re-layouts: 9.68 us -> 9.59 us
  transfers between devices with their start and end apart: 4 -> 4, of which waited for: 3 -> 4; matrix products, arithmetic and copies ran while one was open for 8% -> 9% of each run, Pallas kernels for 0% -> 0%
where the time goes in v1:
time: 256 us; the launch traced here: 255 us
  waiting for transfers between devices  201 us (79%)
  between operations  14.2 us (6%)
  local copies, waits for them, and re-layouts  13.8 us (5%)
  matrix products  11.9 us (5%)
  other arithmetic  8.25 us (3%)
  starting transfers between devices  5.14 us (2%)
    all_gather x1, waiting for transfers between devices, local(): all_gather(state, axis_name=mesh_ax).sum(axis=0)  155 us
    all_gather x1, waiting for transfers between devices, local(): gathered = lax.all_gather(cotangent, 'chan', axis=3, tiled=True)  29.3 us
    ppermute x2, waiting for transfers between devices, from_behind(): lax.ppermute(value, axis, [(source, source + steps) for source in range(i...  17 us
    unnamed x26, local copies, waits for them, and re-layouts  9.59 us
    dot_general x3, matrix products, local(): jnp.einsum('bxzky,bxzcy->kc', stacked, slab, preferred_element_type=jnp.f...  8.07 us
  transfers between devices with their start and end apart: 4, of which 4 were waited for; matrix products, arithmetic and copies ran while one was open for 9% of the time, Pallas kernels for 0%

profile of v1, /device:TPU:2, one launch (start us, length us, event | category | flops | bytes accessed | tf_op | source)
XLA Modules:
  0.0 254.8 jit_solution(3066578206456327360)
XLA Ops:
  7.2 0.0 all-gather.3.cloned.1.call-start
  7.2 0.7 all-gather.3.cloned.1.call-update
  7.9 0.0 all-gather.5.cloned.1.call-start
  7.9 1.8 fusion.64
  9.7 1.7 fusion.60
  11.4 0.0 copy-start.1
  11.4 29.3 %all-gather.3.cloned.1.call-done = bf16[1,2,8,128,512]{4,3,2,1,0:T(8,128)(2,1)} async-done(((bf16[1,2,8,16,512]{4,3,2,1,0:T(8,128)(2,1)}), bf16[1,2,8,128,512]{4,3,2,1,0:T(8,128)(2,1)}) %all-gather.3.cloned.1.call-update) | async-done | bytes 2097168 | tf_op jit(solution)/shard_map/all_gather | solution.py:24
  40.7 1.7 fusion.68
  42.4 0.0 copy-start.2
  42.4 0.0 copy-start
  42.4 3.8 %collective-permute-start.1 = (bf16[1,1,8,128,512]{4,3,2,1,0:T(8,128)(2,1)S(1)}, bf16[1,1,8,128,512]{4,3,2,1,0:T(8,128)(2,1)S(1)}, u32[]{:S(2)}, u32[]{:S(2)}) collective-permute-start(bf16[1,1,8,128,512]{4,3,2,1,0:T(8,128)(2,1)S(1)} %get-tuple-element.2), channel_id=1, source_target_pairs={{0,16},{16,32},{32,48},{48,64},{64,80},{80,96},{96,112},{112,128},... | collective-permute-start | bytes 3145736 | tf_op jit(solution)/shard_map/ppermute | solution.py:12
  46.2 0.0 copy-done.1
  46.2 0.9 fusion.65
  47.2 0.8 fusion.62
  48.0 0.7 constant_dynamic-update-slice_fusion
  48.7 1.3 collective-permute-start
  50.0 0.9 fusion.63
  50.9 0.8 fusion.66
  51.7 0.7 fusion.61
  52.5 0.9 fusion.67
  53.3 0.0 copy-done
  53.3 2.4 fusion.25
  55.8 13.2 %collective-permute-done.1 = bf16[1,1,8,128,512]{4,3,2,1,0:T(8,128)(2,1)S(1)} collective-permute-done((bf16[1,1,8,128,512]{4,3,2,1,0:T(8,128)(2,1)S(1)}, bf16[1,1,8,128,512]{4,3,2,1,0:T(8,128)(2,1)S(1)}, u32[]{:S(2)}, u32[]{:S(2)}) %collective-permute-start.1) | collective-permute-done | bytes 1048608 | tf_op jit(solution)/shard_map/ppermute | solution.py:12
  69.0 0.0 copy-start.4
  69.0 2.8 %fusion.30 = f32[144,128]{1,0:T(8,128)S(1)} fusion(bf16[1,2,8,144,512]{4,3,2,1,0:T(8,128)(2,1)} %fusion.67, bf16[1,1,8,128,512]{4,3,2,1,0:T(8,128)(2,1)S(1)} %get-tuple-element.3, bf16[1,1,8,128,512]{4,3,2,1,0:T(8,128)(2,1)S(1)} %collective-permute-done.1), kind=kOutput, calls=%fused_computation.26 | convolution fusion | flops 303038464 | bytes 4530176 | tf_op jit(solution)/shard_map/bxzky,bxzcy->kc/dot_general | solution.py:42
  71.8 0.0 copy-done.4
  71.8 0.0 copy-start.8
  71.8 3.8 %collective-permute-done = bf16[1,1,8,128,512]{4,3,2,1,0:T(8,128)(2,1)S(1)} collective-permute-done((bf16[1,1,8,128,512]{4,3,2,1,0:T(8,128)(2,1)S(1)}, bf16[1,1,8,128,512]{4,3,2,1,0:T(8,128)(2,1)S(1)}, u32[]{:S(2)}, u32[]{:S(2)}) %collective-permute-start) | collective-permute-done | bytes 1048608 | tf_op jit(solution)/shard_map/ppermute | solution.py:12
  75.6 0.0 copy-done.2
  75.6 0.0 copy-start.6
  75.6 2.8 %fusion.22 = f32[144,128]{1,0:T(8,128)S(1)} fusion(bf16[1,2,8,144,512]{4,3,2,1,0:T(8,128)(2,1)} %fusion.67, bf16[1,1,8,128,512]{4,3,2,1,0:T(8,128)(2,1)S(1)} %collective-permute-done, bf16[1,1,8,128,512]{4,3,2,1,0:T(8,128)(2,1)S(1)} %get-tuple-element.2), kind=kOutput, calls=%fused_computation.24 | convolution fusion | flops 303038464 | bytes 4530176 | tf_op jit(solution)/shard_map/bxzky,bxzcy->kc/dot_general | solution.py:42
  78.5 0.0 copy-done.6
  78.5 0.7 pad_maximum_fusion
  79.2 0.0 all-gather.5.cloned.1.call-update
  79.2 0.0 copy-done.8
  79.2 0.4 fusion.16
  79.6 0.4 fusion.19
  80.1 0.4 fusion.13
  80.5 0.2 fusion.74
  80.7 0.0 copy-start.3
  80.7 0.0 copy-start.7
  80.7 0.4 fusion.72
  81.1 0.0 copy-start.5
  81.1 0.8 copy-done.3
  81.9 0.3 copy-done.7
  82.2 0.4 convolution_bitcast_fusion.4
  82.6 0.0 copy-done.5
  82.6 0.4 convolution_bitcast_fusion.1
  83.1 0.4 convolution_bitcast_fusion.5
  83.5 0.4 convolution_bitcast_fusion.3
  83.9 0.4 convolution_bitcast_fusion.2
  84.3 0.4 convolution_bitcast_fusion
  84.8 0.2 fusion.71
  84.9 0.2 fusion.77
  85.1 0.4 fusion.69
  85.5 0.4 fusion.75
  85.9 3.4 %fusion.59 = bf16[1,2,8,16,512]{4,3,2,1,0:T(8,128)(2,1)} fusion(f32[1,2,8,16,512]{4,3,2,1,0:T(8,128)S(1)} %get-tuple-element.26, f32[1,2,8,16,512]{4,3,2,1,0:T(8,128)S(1)} %get-tuple-element.27, f32[1,2,8,16,512]{4,3,2,1,0:T(8,128)S(1)} %get-tuple-element.25, f32[1,2,8,16,512]{4,3,2,1,0:T(8,128)S(1)} %get-tuple-element.41, ...), kind=kLoop, calls=%fused_computation.77 | loop fusion | flops 3538944 | bytes 14417920 | tf_op jit(solution)/shard_map/convert_element_type | solution.py:52
  89.3 154.5 %all-gather.5.cloned.1.call-done = f32[32,27,16,128]{3,2,1,0:T(8,128)} async-done(((f32[1,27,16,128]{3,2,1,0:T(8,128)}), f32[32,27,16,128]{3,2,1,0:T(8,128)}) %all-gather.5.cloned.1.call-update) | async-done | bytes 7077904 | tf_op jit(solution)/shard_map/all_gather | solution.py:56
  243.8 3.5 %reduce_sum.9 = f32[27,16,128]{2,1,0:T(8,128)S(1)} reduce(f32[32,27,16,128]{3,2,1,0:T(8,128)} %all-gather.5.cloned.1.call-done, f32[]{:T(128)} %constant.0.clone.1), dimensions={0}, to_apply=%region_0.0 | reduce | flops 1714176 | bytes 7299076 | tf_op jit(solution)/shard_map/reduce_sum | solution.py:56
  247.3 0.7 broadcast_multiply_fusion
  (1 shorter events, 0.0 us)
Async XLA Ops:
  7.2 33.5 %all-gather.3.cloned.1.call-start = ((), (), s32[]{:S(2)}) async-start(), calls=%async_computation | async-start | bytes 2359296 | tf_op jit(solution)/shard_map/all_gather | solution.py:24
  7.9 235.9 %all-gather.5.cloned.1.call-start = ((), (), s32[]{:S(2)}) async-start(), calls=%async_computation.1 | async-start | bytes 7299072 | tf_op jit(solution)/shard_map/all_gather | solution.py:56
  11.4 34.8 %copy-start.1 = (bf16[1,2,8,16,512]{4,3,2,1,0:T(8,128)(2,1)S(1)}, bf16[1,2,8,16,512]{4,3,2,1,0:T(8,128)(2,1)}, u32[]{:S(2)}) copy-start(bf16[1,2,8,16,512]{4,3,2,1,0:T(8,128)(2,1)} %param.3) | copy-start | bytes 786436
  42.4 33.2 %copy-start.2 = (bf16[1,1,8,128,512]{4,3,2,1,0:T(8,128)(2,1)}, bf16[1,1,8,128,512]{4,3,2,1,0:T(8,128)(2,1)S(1)}, u32[]{:S(2)}) copy-start(bf16[1,1,8,128,512]{4,3,2,1,0:T(8,128)(2,1)S(1)} %get-tuple-element.2) | copy-start | bytes 3145732
  42.4 10.9 %copy-start = (bf16[1,2,8,128,512]{4,3,2,1,0:T(8,128)(2,1)S(1)}, bf16[1,2,8,128,512]{4,3,2,1,0:T(8,128)(2,1)}, u32[]{:S(2)}) copy-start(bf16[1,2,8,128,512]{4,3,2,1,0:T(8,128)(2,1)} %all-gather.3.cloned.1.call-done) | copy-start | bytes 6291460
  42.4 26.5 %collective-permute-start.1 = (bf16[1,1,8,128,512]{4,3,2,1,0:T(8,128)(2,1)S(1)}, bf16[1,1,8,128,512]{4,3,2,1,0:T(8,128)(2,1)S(1)}, u32[]{:S(2)}, u32[]{:S(2)}) collective-permute-start(bf16[1,1,8,128,512]{4,3,2,1,0:T(8,128)(2,1)S(1)} %get-tuple-element.2), channel_id=1, source_target_pairs={{0,16},{16,32},{32,48},{48,64},{64,80},{80,96},{96,112},{112,128},... | collective-permute-start | bytes 3145736 | tf_op jit(solution)/shard_map/ppermute | solution.py:12
  48.7 26.9 %collective-permute-start = (bf16[1,1,8,128,512]{4,3,2,1,0:T(8,128)(2,1)S(1)}, bf16[1,1,8,128,512]{4,3,2,1,0:T(8,128)(2,1)S(1)}, u32[]{:S(2)}, u32[]{:S(2)}) collective-permute-start(bf16[1,1,8,128,512]{4,3,2,1,0:T(8,128)(2,1)S(1)} %get-tuple-element.3), channel_id=1, source_target_pairs={{16,0},{32,16},{48,32},{64,48},{80,64},{96,80},{112,96},{128,112},... | collective-permute-start | bytes 3145736 | tf_op jit(solution)/shard_map/ppermute | solution.py:12
  69.0 2.8 %copy-start.4 = (bf16[1,1,8,128,512]{4,3,2,1,0:T(8,128)(2,1)}, bf16[1,1,8,128,512]{4,3,2,1,0:T(8,128)(2,1)S(1)}, u32[]{:S(2)}) copy-start(bf16[1,1,8,128,512]{4,3,2,1,0:T(8,128)(2,1)S(1)} %collective-permute-done.1) | copy-start | bytes 3145732
  71.8 7.4 %copy-start.8 = (bf16[27,16,128]{2,1,0:T(8,128)(2,1)S(1)}, bf16[27,16,128]{2,1,0:T(8,128)(2,1)}, u32[]{:S(2)}) copy-start(bf16[27,16,128]{2,1,0:T(8,128)(2,1)} %param.5) | copy-start | bytes 331780
  75.6 2.8 %copy-start.6 = (bf16[1,1,8,128,512]{4,3,2,1,0:T(8,128)(2,1)}, bf16[1,1,8,128,512]{4,3,2,1,0:T(8,128)(2,1)S(1)}, u32[]{:S(2)}) copy-start(bf16[1,1,8,128,512]{4,3,2,1,0:T(8,128)(2,1)S(1)} %collective-permute-done) | copy-start | bytes 3145732
  80.7 1.2 copy-start.3
  80.7 1.5 copy-start.7
  81.1 1.6 copy-start.5
Sparse Core Ops, SparseCore 0:
  9.8 30.8 all-gather.2
  79.3 164.4 all-gather.4
